TPU v7x, 32 devices: a whole 2x2x4 slice. The times are simulated.
32 devices in a mesh: group: 2 (over x), tm: 2 (over core), height: 8 (over z, y).
Axes of the slice: x: 2, y: 2, z: 4, core: 2. Of those that a mesh axis runs over, the one named last changes fastest.
Arguments:
- frames: bfloat16 [8, 16, 128, 384], P(('group', 'tm'), 'height'), parts along dimension 0, may hold values from -20 to 20
- earlier: int32 [8, 2], P(('group', 'tm')), parts along dimension 0, may hold values from -1 to 3, as said below
- gain_conv: float32 [384], replicated, may hold values from 0.1 to 1.9
- conv_weight: bfloat16 [3, 3, 3, 384, 384], replicated, may hold values from -0.0625 to 0.0625
- conv_bias: float32 [384], replicated, may hold values from -3 to 3
- gain_attn: float32 [384], replicated, may hold values from 0.1 to 1.9
- query_weight: bfloat16 [384, 384], replicated
- key_weight: bfloat16 [384, 384], replicated
- value_weight: bfloat16 [384, 384], replicated, may hold values from -0.3125 to 0.3125
- out_weight: bfloat16 [384, 384], replicated, may hold values from -0.3125 to 0.3125
Outputs:
- encoded: bfloat16 [8, 16, 128, 384], P(('group', 'tm'), 'height'), parts along dimension 0
There are 2 independent parts, one for each index of `group`. A program takes and returns all parts, laid end to end along the dimension named above; an argument that names none is the same for every part. Nothing has to cross between parts.
Inputs may be any that keep to these rules, and one draw needn't show every extreme that they name: Row i names the spans whose frames come two back and one back before span i's frame in the same clip, -1 where the clip has no such frame; spans of a clip may lie on either index of tm, in an order drawn from the seed. earlier[i, 0] is -1 whenever earlier[i, 1] is -1. Every span is named at most once in each column.
All inputs are finite; a program needn't handle non-finite values.
Results may differ from a plain program's by a relative error of at most 0.014.
Values may be sent and summed in bfloat16 or wider, within the bound.
No kernel may reach another device: no remote copies, remote signals or barrier semaphores. Data moves between devices by JAX's collectives and lax.ppermute only.
A program may use at most 128 MiB of HBM per device.

v0:
```python
import jax
import jax.numpy as jnp
from jax import lax
from jax.sharding import PartitionSpec as P


def padded_2(cells, sides, width):
    for axis, dim in sides:
        count = lax.axis_size(axis)
        ends = count - 1
        head = lax.slice_in_dim(cells, 0, width, axis=dim)
        tail = lax.slice_in_dim(cells, cells.shape[dim] - width, cells.shape[dim], axis=dim)
        cells = jnp.concatenate(
            [
                lax.ppermute(tail, axis, [(i, (i + 1) % count) for i in range(ends)]),
                cells,
                lax.ppermute(head, axis, [((i + 1) % count, i) for i in range(ends)]),
            ],
            axis=dim,
        )
    return cells


def rms_scaled(frames, gain):
    widened = frames.astype(jnp.float32)
    mean_square = jnp.mean(widened * widened, axis=-1, keepdims=True)
    return widened * lax.rsqrt(mean_square + 1e-06) * gain


def shards(
    frames,
    earlier,
    gain_conv,
    conv_weight,
    conv_bias,
    gain_attn,
    query_weight,
    key_weight,
    value_weight,
    out_weight,
):
    span_count, row_count, col_count, channels = frames.shape
    activated = jax.nn.silu(rms_scaled(frames, gain_conv)).astype(jnp.bfloat16)
    rimmed = padded_2(activated, (("height", 1),), 1)
    gathered = lax.all_gather(rimmed, "tm", axis=0, tiled=True)
    border = ((0, 0), (0, 0), (1, 1), (0, 0))
    padded = jnp.pad(rimmed, border)
    gathered = jnp.pad(gathered, border)
    back_two = jnp.take(gathered, jnp.maximum(earlier[:, 0], 0), axis=0)
    back_one = jnp.take(gathered, jnp.maximum(earlier[:, 1], 0), axis=0)
    present_two = (earlier[:, 0] >= 0)[:, None, None, None]
    present_one = (earlier[:, 1] >= 0)[:, None, None, None]
    back_two = jnp.where(present_two, back_two, jnp.zeros_like(back_two))
    back_one = jnp.where(present_one, back_one, jnp.zeros_like(back_one))
    window = jnp.stack([back_two, back_one, padded], axis=1)
    score_scale = 1.0 / channels**0.5

    def conv_span(span_window, span):
        accum = jnp.zeros((row_count, col_count, channels), jnp.float32)
        for tap_t in range(3):
            for tap_y in range(3):
                for tap_x in range(3):
                    sliced = span_window[
                        tap_t, tap_y : tap_y + row_count, tap_x : tap_x + col_count
                    ]
                    accum = accum + jnp.einsum(
                        "hwc,cd->hwd",
                        sliced,
                        conv_weight[tap_t, tap_y, tap_x],
                        preferred_element_type=jnp.float32,
                    )
        mixed = (frames[span].astype(jnp.float32) + accum + conv_bias).astype(jnp.bfloat16)
        normed = rms_scaled(mixed, gain_attn).astype(jnp.bfloat16)
        return (mixed, normed.reshape(row_count * col_count, channels))

    def attend_span(mixed, tokens, tokens_all):
        queries = jnp.dot(tokens, query_weight, preferred_element_type=jnp.float32).astype(
            jnp.bfloat16
        )
        keys_all = jnp.dot(tokens_all, key_weight, preferred_element_type=jnp.float32).astype(
            jnp.bfloat16
        )
        values_all = jnp.dot(tokens_all, value_weight, preferred_element_type=jnp.float32).astype(
            jnp.bfloat16
        )
        scores = (
            jnp.einsum("qc,kc->qk", queries, keys_all, preferred_element_type=jnp.float32)
            * score_scale
        )
        peaks = jnp.max(scores, axis=-1, keepdims=True)
        weights_exp = jnp.exp(scores - peaks)
        totals = jnp.sum(weights_exp, axis=-1, keepdims=True)
        summed = jnp.dot(
            weights_exp.astype(jnp.bfloat16), values_all, preferred_element_type=jnp.float32
        )
        attended = (summed / totals).astype(jnp.bfloat16)
        projected = jnp.dot(attended, out_weight, preferred_element_type=jnp.float32)
        encoded = mixed.astype(jnp.float32) + projected.reshape(row_count, col_count, channels)
        return encoded.astype(jnp.bfloat16)

    outputs = []
    pending = None
    span_window = window[0]
    for span in range(span_count):
        mixed, tokens = conv_span(span_window, span)
        if span + 1 < span_count:
            tokens, span_window = lax.optimization_barrier((tokens, window[span + 1]))
        tokens_all = lax.all_gather(tokens, "height", axis=0, tiled=True)
        if pending is not None:
            mixed, tokens, pending = lax.optimization_barrier((mixed, tokens, pending))
            outputs.append(attend_span(*pending))
        pending = (mixed, tokens, tokens_all)
    outputs.append(attend_span(*pending))
    return jnp.stack(outputs, axis=0)


def solution(mesh):
    in_specs = (
        P(("group", "tm"), "height", None, None),
        P(("group", "tm"), None),
        P(),
        P(),
        P(),
        P(),
        P(),
        P(),
        P(),
        P(),
    )
    out_specs = P(("group", "tm"), "height", None, None)
    return jax.shard_map(shards, mesh=mesh, in_specs=in_specs, out_specs=out_specs, check_vma=False)
```

profile of v0, /device:TPU:0, one launch (start us, length us, event | category | flops | bytes accessed | tf_op | source)
XLA Modules:
  0.0 183.2 jit_solution(11251715739805948440)
XLA Ops:
  6.5 1.2 fusion.22
  7.8 1.3 fusion.29
  9.1 4.9 %collective-permute-start = (bf16[2,1,128,384]{3,2,1,0:T(8,128)(2,1)S(1)}, bf16[2,1,128,384]{3,2,1,0:T(8,128)(2,1)S(1)}, u32[]{:S(2)}, u32[]{:S(2)}) collective-permute-start(bf16[2,1,128,384]{3,2,1,0:T(8,128)(2,1)S(1)} %get-tuple-element.26), channel_id=1, source_target_pairs={{0,1},{1,2},{2,3},{3,4},{4,5},{5,6},{6,7},{8,9},{9,10},{10,11},{11... | collective-permute-start | bytes 589832 | tf_op jit(solution)/shard_map/ppermute | solution.py:15
  14.0 1.3 collective-permute-start.1
  15.3 2.9 %collective-permute-done = bf16[2,1,128,384]{3,2,1,0:T(8,128)(2,1)S(1)} collective-permute-done((bf16[2,1,128,384]{3,2,1,0:T(8,128)(2,1)S(1)}, bf16[2,1,128,384]{3,2,1,0:T(8,128)(2,1)S(1)}, u32[]{:S(2)}, u32[]{:S(2)}) %collective-permute-start) | collective-permute-done | bytes 196640 | tf_op jit(solution)/shard_map/ppermute | solution.py:15
  18.2 4.1 %collective-permute-done.1 = bf16[2,1,128,384]{3,2,1,0:T(8,128)(2,1)S(1)} collective-permute-done((bf16[2,1,128,384]{3,2,1,0:T(8,128)(2,1)S(1)}, bf16[2,1,128,384]{3,2,1,0:T(8,128)(2,1)S(1)}, u32[]{:S(2)}, u32[]{:S(2)}) %collective-permute-start.1) | collective-permute-done | bytes 196640 | tf_op jit(solution)/shard_map/ppermute | solution.py:17
  22.3 1.0 pad_maximum_fusion.1
  23.8 1.3 pad_bitcast_fusion
  25.1 10.4 %all-gather.4.cloned.1.call-done = bf16[4,4,128,384]{3,2,1,0:T(8,128)(2,1)} async-done(((bf16[2,4,128,384]{3,2,1,0:T(8,128)(2,1)}), bf16[4,4,128,384]{3,2,1,0:T(8,128)(2,1)}) %all-gather.4.cloned.1.call-update) | async-done | bytes 1572880 | tf_op jit(solution)/shard_map/all_gather | solution.py:45
  35.5 1.9 %pad.8 = bf16[4,4,130,384]{3,2,1,0:T(8,128)(2,1)S(1)} pad(bf16[4,4,128,384]{3,2,1,0:T(8,128)(2,1)} %all-gather.4.cloned.1.call-done, bf16[]{:T(256)} %constant.9.clone.1), padding=0_0x0_0x1_1x0_0 | pad | bytes 3170306 | tf_op jit(solution)/shard_map/jit(_pad)/pad | solution.py:48
  37.5 1.6 gather_fusion.1
  39.0 1.6 gather_fusion
  40.6 1.5 fusion.20
  42.3 0.3 pad_maximum_fusion
  42.9 1.5 fusion.38
  44.5 1.2 convolution_add_fusion.51
  48.0 0.3 convolution_add_fusion.42
  48.3 0.3 convolution_add_fusion.41
  48.8 0.3 convolution_add_fusion.39
  49.7 0.3 convolution_add_fusion.36
  49.9 0.3 convolution_add_fusion.35
  51.6 0.3 convolution_add_fusion.29
  52.6 0.4 fusion.30
  53.0 0.8 fusion.32
  53.8 1.2 fusion.36
  55.1 1.2 convolution_add_fusion.25
  56.3 1.2 convolution_add_fusion.24
  57.6 1.2 convolution_add_fusion.23
  58.8 1.2 convolution_add_fusion.22
  60.0 1.2 convolution_add_fusion.21
  61.3 1.2 convolution_add_fusion.20
  62.5 1.2 convolution_add_fusion.19
  63.8 1.2 convolution_add_fusion.18
  65.0 1.2 convolution_add_fusion.17
  66.2 1.2 convolution_add_fusion.16
  67.5 1.2 convolution_add_fusion.15
  68.7 1.2 convolution_add_fusion.14
  69.9 1.2 convolution_add_fusion.13
  71.2 1.2 convolution_add_fusion.12
  72.4 1.2 convolution_add_fusion.11
  73.7 1.4 convolution_add_fusion.10
  75.1 1.2 convolution_add_fusion.9
  76.4 1.2 convolution_add_fusion.8
  77.6 1.2 convolution_add_fusion.7
  78.9 1.2 convolution_add_fusion.6
  80.1 1.2 convolution_add_fusion.5
  81.4 1.2 convolution_add_fusion.4
  82.6 1.2 convolution_add_fusion.3
  83.9 1.3 convolution_add_fusion.2
  85.2 1.2 convolution_add_fusion.1
  86.4 1.4 fusion.33
  87.8 0.8 fusion.35
  88.6 33.3 %all-gather.6.cloned.1.call-done = bf16[2048,384]{1,0:T(8,128)(2,1)} async-done(((bf16[256,384]{1,0:T(8,128)(2,1)}), bf16[2048,384]{1,0:T(8,128)(2,1)}) %all-gather.6.cloned.1.call-update) | async-done | bytes 1572880 | tf_op jit(solution)/shard_map/all_gather | solution.py:108
  122.2 3.1 %fusion.204 = (f32[256]{0:T(256)S(1)}, f32[256,2048]{1,0:T(8,128)S(1)}) fusion(bf16[256,384]{1,0:T(8,128)(2,1)S(1)} %convolution_convert_fusion.5, bf16[2048,384]{1,0:T(8,128)(2,1)} %all-gather.6.cloned.1.call-done, bf16[384,384]{1,0:T(8,128)(2,1)S(1)} %copy-done), kind=kOutput, calls=%fused_computation.322 | convolution fusion | flops 1008467712 | bytes 4162560 | tf_op jit(solution)/shard_map/qc,kc->qk/dot_general | solution.py:87
  125.3 0.4 fusion
  125.8 0.5 copy-done.3
  126.3 1.0 convolution_convert_fusion.4
  127.2 3.1 %fusion.15 = bf16[256,384]{1,0:T(8,128)(2,1)S(1)} fusion(bf16[2048,384]{1,0:T(8,128)(2,1)} %all-gather.6.cloned.1.call-done, bf16[384,384]{1,0:T(8,128)(2,1)} %param.20, f32[256,2048]{1,0:T(8,128)S(1)} %get-tuple-element.35, f32[256]{0:T(256)S(1)} %get-tuple-element.34, f32[256]{0:T(256)S(1)} %fusion), kind=kOutput, calls=%fused_computation.82 | convolution fusion | flops 1008664576 | bytes 4163584 | tf_op jit(solution)/shard_map/dot_general | solution.py:93
  130.7 36.5 %all-gather.8.cloned.1.call-done = bf16[2048,384]{1,0:T(8,128)(2,1)} async-done(((bf16[256,384]{1,0:T(8,128)(2,1)}), bf16[2048,384]{1,0:T(8,128)(2,1)}) %all-gather.8.cloned.1.call-update) | async-done | bytes 1572880 | tf_op jit(solution)/shard_map/all_gather | solution.py:108
  167.1 3.3 %fusion.203 = (f32[256]{0:T(256)S(1)}, f32[256,2048]{1,0:T(8,128)S(1)}) fusion(bf16[256,384]{1,0:T(8,128)(2,1)} %convolution_convert_fusion.4, bf16[2048,384]{1,0:T(8,128)(2,1)} %all-gather.8.cloned.1.call-done, bf16[384,384]{1,0:T(8,128)(2,1)S(1)} %copy-done), kind=kOutput, calls=%fused_computation.321 | convolution fusion | flops 1008467712 | bytes 4162560 | tf_op jit(solution)/shard_map/qc,kc->qk/dot_general | solution.py:87
  170.4 0.4 fusion.2
  170.8 3.8 %fusion.13 = bf16[256,384]{1,0:T(8,128)(2,1)} fusion(bf16[2048,384]{1,0:T(8,128)(2,1)} %all-gather.8.cloned.1.call-done, bf16[384,384]{1,0:T(8,128)(2,1)} %param.20, f32[256,2048]{1,0:T(8,128)S(1)} %get-tuple-element.33, f32[256]{0:T(256)S(1)} %get-tuple-element.32, f32[256]{0:T(256)S(1)} %fusion.2), kind=kOutput, calls=%fused_computation.80 | convolution fusion | flops 1008664576 | bytes 4163584 | tf_op jit(solution)/shard_map/dot_general | solution.py:93
  174.6 1.2 fusion.206
  175.9 0.8 pad_maximum_fusion.2
  (64 shorter events, 6.7 us)
Async XLA Ops:
  6.5 115.6 %copy-start = (bf16[384,384]{1,0:T(8,128)(2,1)S(1)}, bf16[384,384]{1,0:T(8,128)(2,1)}, u32[]{:S(2)}) copy-start(bf16[384,384]{1,0:T(8,128)(2,1)} %param.19) | copy-start | bytes 884740
  6.5 16.8 %copy-start.7 = (s32[2,2]{1,0:T(2,128)S(1)}, s32[2,2]{1,0:T(2,128)}, u32[]{:S(2)}) copy-start(s32[2,2]{1,0:T(2,128)} %param.13) | copy-start | bytes 52
  6.5 29.0 %all-gather.4.cloned.1.call-start = ((), (), s32[]{:S(2)}) async-start(), calls=%async_computation | async-start | bytes 2359296 | tf_op jit(solution)/shard_map/all_gather | solution.py:45
  9.1 9.1 %collective-permute-start = (bf16[2,1,128,384]{3,2,1,0:T(8,128)(2,1)S(1)}, bf16[2,1,128,384]{3,2,1,0:T(8,128)(2,1)S(1)}, u32[]{:S(2)}, u32[]{:S(2)}) collective-permute-start(bf16[2,1,128,384]{3,2,1,0:T(8,128)(2,1)S(1)} %get-tuple-element.26), channel_id=1, source_target_pairs={{0,1},{1,2},{2,3},{3,4},{4,5},{5,6},{6,7},{8,9},{9,10},{10,11},{11... | collective-permute-start | bytes 589832 | tf_op jit(solution)/shard_map/ppermute | solution.py:15
  14.0 8.3 %collective-permute-start.1 = (bf16[2,1,128,384]{3,2,1,0:T(8,128)(2,1)S(1)}, bf16[2,1,128,384]{3,2,1,0:T(8,128)(2,1)S(1)}, u32[]{:S(2)}, u32[]{:S(2)}) collective-permute-start(bf16[2,1,128,384]{3,2,1,0:T(8,128)(2,1)S(1)} %get-tuple-element.27), channel_id=1, source_target_pairs={{1,0},{2,1},{3,2},{4,3},{5,4},{6,5},{7,6},{9,8},{10,9},{11,10},{12... | collective-permute-start | bytes 589832 | tf_op jit(solution)/shard_map/ppermute | solution.py:17
  23.3 98.6 %all-gather.6.cloned.1.call-start = ((), (), s32[]{:S(2)}) async-start(), calls=%async_computation.1 | async-start | bytes 1769472 | tf_op jit(solution)/shard_map/all_gather | solution.py:108
  40.6 1.5 copy-start.1
  40.6 5.1 %slice-start = ((s8[7962624]{0:T(1024)(128)(4,1)}), s8[4194304]{0:T(1024)(128)(4,1)S(1)}, s32[]{:S(2)}) async-start(s8[7962624]{0:T(1024)(128)(4,1)} %bitcast.403), calls=%async_computation.3 | async-start | bytes 8388608
  42.3 3.4 %slice-start.1 = ((s8[7962624]{0:T(1024)(128)(4,1)}), s8[3768320]{0:T(1024)(128)(4,1)S(1)}, s32[]{:S(2)}) async-start(s8[7962624]{0:T(1024)(128)(4,1)} %bitcast.403), calls=%async_computation.4 | async-start | bytes 7536640
  51.6 1.0 copy-start.4
  51.6 1.0 copy-start.9
  51.9 1.1 copy-start.8
  76.4 90.8 %all-gather.8.cloned.1.call-start = ((), (), s32[]{:S(2)}) async-start(), calls=%async_computation.2 | async-start | bytes 1769472 | tf_op jit(solution)/shard_map/all_gather | solution.py:108
  83.8 38.1 %copy-start.2 = (bf16[2,128,384]{2,1,0:T(8,128)(2,1)S(1)}, bf16[2,128,384]{2,1,0:T(8,128)(2,1)}, u32[]{:S(2)}) copy-start(bf16[2,128,384]{2,1,0:T(8,128)(2,1)} %fusion.32) | copy-start | bytes 589828
  83.8 38.1 %copy-start.6 = (bf16[384,384]{1,0:T(8,128)(2,1)S(1)}, bf16[384,384]{1,0:T(8,128)(2,1)}, u32[]{:S(2)}) copy-start(bf16[384,384]{1,0:T(8,128)(2,1)} %param.18) | copy-start | bytes 884740
  125.3 0.9 copy-start.3
  127.2 3.2 %copy-start.5 = (bf16[384,384]{1,0:T(8,128)(2,1)S(1)}, bf16[384,384]{1,0:T(8,128)(2,1)}, u32[]{:S(2)}) copy-start(bf16[384,384]{1,0:T(8,128)(2,1)} %param.21) | copy-start | bytes 884740
Sparse Core Ops, SparseCore 0:
  23.4 12.0 all-gather.3
  76.5 45.3 all-gather.5
  124.1 42.9 all-gather.7
where the time goes:
time: 185 us; the launch traced here: 183 us
  waiting for transfers between devices  87.1 us (47%)
  matrix products  59.4 us (32%)
  between operations  13.8 us (7%)
  other arithmetic  9.3 us (5%)
  local copies, waits for them, and re-layouts  7.41 us (4%)
  starting transfers between devices  6.26 us (3%)
    all_gather x2, waiting for transfers between devices, shards(): tokens_all = lax.all_gather(tokens, 'height', axis=0, tiled=True)  69.7 us
    dot_general x54, matrix products, conv_span(): jnp.einsum('hwc,cd->hwd', sliced, conv_weight[tap_t, tap_y, tap_x], prefe...  43.3 us
    all_gather x1, waiting for transfers between devices, shards(): gathered = lax.all_gather(rimmed, 'tm', axis=0, tiled=True)  10.4 us
    dot_general x2, matrix products, attend_span(): jnp.dot(weights_exp.astype(jnp.bfloat16), values_all, preferred_element_t...  6.95 us
    dot_general x2, matrix products, attend_span(): jnp.einsum('qc,kc->qk', queries, keys_all, preferred_element_type=jnp.flo...  6.41 us
    ppermute x1, starting transfers between devices, padded_2(): lax.ppermute(tail, axis, [(i, (i + 1) % count) for i in range(ends)])  4.88 us
    ppermute x1, waiting for transfers between devices, padded_2(): lax.ppermute(head, axis, [((i + 1) % count, i) for i in range(ends)])  4.07 us
  transfers between devices with their start and end apart: 5, of which 5 were waited for; matrix products, arithmetic and copies ran while one was open for 12% of the time, Pallas kernels for 0%

commit v1 on v0

--- a/solution.py
+++ b/solution.py
@@ -2,6 +2,27 @@
 import jax.numpy as jnp
 from jax import lax
 from jax.sharding import PartitionSpec as P
+
+
+def collect(value, axis, dim):
+    size, index, span = (lax.axis_size(axis), lax.axis_index(axis), value.shape[dim])
+    forward = [(i, (i + 1) % size) for i in range(size)]
+    left = [(i, (i - 1) % size) for i in range(size)]
+    out = jnp.zeros((*value.shape[:dim], size * span, *value.shape[dim + 1 :]), value.dtype)
+    out = lax.dynamic_update_slice_in_dim(out, value, index * span, axis=dim)
+    from_left = from_right = value
+    half = size // 2
+    for step in range(1, half + 1):
+        from_left = lax.ppermute(from_left, axis, forward)
+        out = lax.dynamic_update_slice_in_dim(
+            out, from_left, (index - step) % size * span, axis=dim
+        )
+        if step < size - half:
+            from_right = lax.ppermute(from_right, axis, left)
+            out = lax.dynamic_update_slice_in_dim(
+                out, from_right, (index + step) % size * span, axis=dim
+            )
+    return out
 
 
 def padded_2(cells, sides, width):
@@ -105,7 +126,7 @@
         mixed, tokens = conv_span(span_window, span)
         if span + 1 < span_count:
             tokens, span_window = lax.optimization_barrier((tokens, window[span + 1]))
-        tokens_all = lax.all_gather(tokens, "height", axis=0, tiled=True)
+        tokens_all = collect(tokens, "height", 0)
         if pending is not None:
             mixed, tokens, pending = lax.optimization_barrier((mixed, tokens, pending))
             outputs.append(attend_span(*pending))

time: 185 us -> 146 us (0.79)
  waiting for transfers between devices: 87.1 us -> 33.1 us
  starting transfers between devices: 6.26 us -> 36.4 us
  matrix products: 59.4 us -> 31.6 us
  local copies, waits for them, and re-layouts: 7.41 us -> 22.2 us
    all_gather x2 -> x0, waiting for transfers between devices: 69.7 us -> none  [shards(): tokens_all = lax.all_gather(tokens, 'height', axis=0, tiled=True)]
    ppermute x0 -> x14, starting transfers between devices: none -> 30.3 us  [the longest x6 23.3 us: collect(): from_right = lax.ppermute(from_right, axis, left)]
    dot_general x54, matrix products: 43.3 us -> 17.2 us  [conv_span(): jnp.einsum('hwc,cd->hwd', sliced, conv_weight[tap_t, tap_y, tap_x], prefe...]
    ppermute x0 -> x14, waiting for transfers between devices: none -> 15.2 us  [the longest x6 11.2 us: collect(): from_right = lax.ppermute(from_right, axis, left)]
    dynamic_update_slice x0 -> x16, local copies, waits for them, and re-layouts: none -> 13 us  [the longest x8 7.47 us: collect(): lax.dynamic_update_slice_in_dim(out, from_left, (index - step) % size * s...]
    another operation x0 -> x2, local copies, waits for them, and re-layouts: none -> 2.56 us
  transfers between devices with their start and end apart: 5 -> 17, of which waited for: 5 -> 8; matrix products, arithmetic and copies ran while one was open for 12% -> 21% of each run, Pallas kernels for 0% -> 0%
where the time goes in v1:
time: 146 us
  starting transfers between devices  36.4 us (25%)
  waiting for transfers between devices  33.1 us (23%)
  matrix products  31.6 us (22%)
  local copies, waits for them, and re-layouts  22.2 us (15%)
  between operations  14.2 us (10%)
  other arithmetic  7.93 us (5%)
    ppermute x6, starting transfers between devices, collect(): from_right = lax.ppermute(from_right, axis, left)  23.3 us
    dot_general x54, matrix products, conv_span(): jnp.einsum('hwc,cd->hwd', sliced, conv_weight[tap_t, tap_y, tap_x], prefe...  17.2 us
    ppermute x6, waiting for transfers between devices, collect(): from_right = lax.ppermute(from_right, axis, left)  11.2 us
    all_gather x1, waiting for transfers between devices, shards(): gathered = lax.all_gather(rimmed, 'tm', axis=0, tiled=True)  10.9 us
    dynamic_update_slice x8, local copies, waits for them, and re-layouts, collect(): lax.dynamic_update_slice_in_dim(out, from_left, (index - step) % size * s...  7.47 us
    ppermute x8, starting transfers between devices, collect(): from_left = lax.ppermute(from_left, axis, forward)  6.92 us
    dot_general x2, matrix products, attend_span(): jnp.einsum('qc,kc->qk', queries, keys_all, preferred_element_type=jnp.flo...  6.42 us
    dot_general x2, matrix products, attend_span(): jnp.dot(weights_exp.astype(jnp.bfloat16), values_all, preferred_element_t...  6.27 us
  transfers between devices with their start and end apart: 17, of which 8 were waited for; matrix products, arithmetic and copies ran while one was open for 21% of the time, Pallas kernels for 0%

profile of v1, /device:TPU:0, one launch (start us, length us, event | category | flops | bytes accessed | tf_op | source)
XLA Modules:
  0.0 145.5 jit_solution(12430079028841573024)
XLA Ops:
  6.5 1.2 fusion.22
  7.7 1.3 fusion.29
  9.1 4.9 %collective-permute-start = (bf16[2,1,128,384]{3,2,1,0:T(8,128)(2,1)S(1)}, bf16[2,1,128,384]{3,2,1,0:T(8,128)(2,1)S(1)}, u32[]{:S(2)}, u32[]{:S(2)}) collective-permute-start(bf16[2,1,128,384]{3,2,1,0:T(8,128)(2,1)S(1)} %get-tuple-element.26), channel_id=1, source_target_pairs={{0,1},{1,2},{2,3},{3,4},{4,5},{5,6},{6,7},{8,9},{9,10},{10,11},{11... | collective-permute-start | bytes 589832 | tf_op jit(solution)/shard_map/ppermute | solution.py:36
  14.0 1.3 collective-permute-start.1
  15.3 2.9 %collective-permute-done = bf16[2,1,128,384]{3,2,1,0:T(8,128)(2,1)S(1)} collective-permute-done((bf16[2,1,128,384]{3,2,1,0:T(8,128)(2,1)S(1)}, bf16[2,1,128,384]{3,2,1,0:T(8,128)(2,1)S(1)}, u32[]{:S(2)}, u32[]{:S(2)}) %collective-permute-start) | collective-permute-done | bytes 196640 | tf_op jit(solution)/shard_map/ppermute | solution.py:36
  18.2 4.1 %collective-permute-done.1 = bf16[2,1,128,384]{3,2,1,0:T(8,128)(2,1)S(1)} collective-permute-done((bf16[2,1,128,384]{3,2,1,0:T(8,128)(2,1)S(1)}, bf16[2,1,128,384]{3,2,1,0:T(8,128)(2,1)S(1)}, u32[]{:S(2)}, u32[]{:S(2)}) %collective-permute-start.1) | collective-permute-done | bytes 196640 | tf_op jit(solution)/shard_map/ppermute | solution.py:38
  22.3 1.0 pad_maximum_fusion.1
  23.8 0.6 copy-done.1
  24.6 10.9 %all-gather.2.cloned.1.call-done = bf16[4,4,128,384]{3,2,1,0:T(8,128)(2,1)} async-done(((bf16[2,4,128,384]{3,2,1,0:T(8,128)(2,1)}), bf16[4,4,128,384]{3,2,1,0:T(8,128)(2,1)}) %all-gather.2.cloned.1.call-update) | async-done | bytes 1572880 | tf_op jit(solution)/shard_map/all_gather | solution.py:66
  35.5 1.9 %pad.8 = bf16[4,4,130,384]{3,2,1,0:T(8,128)(2,1)S(1)} pad(bf16[4,4,128,384]{3,2,1,0:T(8,128)(2,1)} %all-gather.2.cloned.1.call-done, bf16[]{:T(256)} %constant.93.clone.1), padding=0_0x0_0x1_1x0_0 | pad | bytes 3170306 | tf_op jit(solution)/shard_map/jit(_pad)/pad | solution.py:69
  37.4 1.6 %gather_fusion.1 = bf16[2,4,130,384]{3,2,1,0:T(8,128)(2,1)} fusion(bf16[4,4,130,384]{3,2,1,0:T(8,128)(2,1)S(1)} %pad.8, s32[1024]{0:T(1024)S(1)} %pad_clamp_fusion), kind=kCustom, calls=%fused_computation.1.clone | custom fusion | bytes 1597448 | tf_op jit(solution)/shard_map/jit(_take)/gather | solution.py:71
  39.0 1.6 %gather_fusion = bf16[2,4,130,384]{3,2,1,0:T(8,128)(2,1)} fusion(bf16[4,4,130,384]{3,2,1,0:T(8,128)(2,1)S(1)} %pad.8, s32[1024]{0:T(1024)S(1)} %pad_clamp_fusion.1), kind=kCustom, calls=%fused_computation.clone | custom fusion | bytes 1597448 | tf_op jit(solution)/shard_map/jit(_take)/gather | solution.py:70
  40.6 1.5 %fusion.20 = bf16[2,1,4,130,384]{4,3,2,1,0:T(8,128)(2,1)S(1)} fusion(bf16[2,4,130,384]{3,2,1,0:T(8,128)(2,1)} %gather_fusion.1, pred[2]{0:T(512)(128)(4,1)S(1)} %get-tuple-element.38, pred[2]{0:T(512)(128)(4,1)S(1)} %get-tuple-element.21), kind=kLoop, calls=%fused_computation.88 | loop fusion | flops 798720 | bytes 1597444 | tf_op jit(solution)/shard_map/stack | solution.py:76
  42.3 0.3 pad_maximum_fusion
  42.9 1.5 %fusion.38 = f32[2,128,384]{2,1,0:T(8,128)S(1)} fusion(bf16[3,3,3,384,384]{4,3,2,1,0:T(8,128)(2,1)} %param.15, bf16[3,4,130,384]{3,2,1,0:T(8,128)(2,1)S(1)} %get-tuple-element.25), kind=kOutput, calls=%fused_computation.116 | convolution fusion | flops 75497472 | bytes 884736 | tf_op jit(solution)/shard_map/hwc,cd->hwd/dot_general | solution.py:87
  44.5 1.2 convolution_add_fusion.51
  48.3 0.3 convolution_add_fusion.41
  49.9 0.3 convolution_add_fusion.35
  51.6 0.3 convolution_add_fusion.29
  52.5 0.4 copy-done.3
  52.9 0.4 fusion.30
  53.5 1.8 %collective-permute-start.2 = (bf16[256,384]{1,0:T(8,128)(2,1)S(1)}, bf16[256,384]{1,0:T(8,128)(2,1)S(1)}, u32[]{:S(2)}, u32[]{:S(2)}) collective-permute-start(bf16[256,384]{1,0:T(8,128)(2,1)S(1)} %bitcast.405), channel_id=1, source_target_pairs={{0,1},{1,2},{2,3},{3,4},{4,5},{5,6},{6,7},{7,0},{8,9},{9,10},{10,1... | collective-permute-start | bytes 589832 | tf_op jit(solution)/shard_map/ppermute | solution.py:16
  55.2 3.0 %collective-permute-start.3 = (bf16[256,384]{1,0:T(8,128)(2,1)S(1)}, bf16[256,384]{1,0:T(8,128)(2,1)S(1)}, u32[]{:S(2)}, u32[]{:S(2)}) collective-permute-start(bf16[256,384]{1,0:T(8,128)(2,1)S(1)} %bitcast.406), channel_id=1, source_target_pairs={{0,7},{1,0},{2,1},{3,2},{4,3},{5,4},{6,5},{7,6},{8,15},{9,8},{10,9... | collective-permute-start | bytes 589832 | tf_op jit(solution)/shard_map/ppermute | solution.py:21
  61.3 0.3 convolution_add_fusion.15
  62.7 0.3 convolution_add_fusion.10
  63.0 0.3 convolution_add_fusion.9
  65.5 0.4 fusion.33
  66.1 4.7 %collective-permute-start.10 = (bf16[256,384]{1,0:T(8,128)(2,1)S(1)}, bf16[256,384]{1,0:T(8,128)(2,1)S(1)}, u32[]{:S(2)}, u32[]{:S(2)}) collective-permute-start(bf16[256,384]{1,0:T(8,128)(2,1)S(1)} %bitcast.410), channel_id=1, source_target_pairs={{0,7},{1,0},{2,1},{3,2},{4,3},{5,4},{6,5},{7,6},{8,15},{9,8},{10,9... | collective-permute-start | bytes 589832 | tf_op jit(solution)/shard_map/ppermute | solution.py:21
  70.8 1.3 broadcast.101.clone.1
  72.1 0.7 constant_dynamic-update-slice_fusion.15
  72.8 1.3 broadcast.101.clone
  74.1 0.7 constant_dynamic-update-slice_fusion.7
  74.8 4.7 %collective-permute-start.5 = (bf16[256,384]{1,0:T(8,128)(2,1)S(1)}, bf16[256,384]{1,0:T(8,128)(2,1)S(1)}, u32[]{:S(2)}, u32[]{:S(2)}) collective-permute-start(bf16[256,384]{1,0:T(8,128)(2,1)S(1)} %collective-permute-done.3), channel_id=1, source_target_pairs={{0,7},{1,0},{2,1},{3,2},{4,3},{5,4},{6,5},{7,6},{8,15},{9,8},{10,9... | collective-permute-start | bytes 589832 | tf_op jit(solution)/shard_map/ppermute | solution.py:21
  79.6 2.5 %collective-permute-start.11 = (bf16[256,384]{1,0:T(8,128)(2,1)S(1)}, bf16[256,384]{1,0:T(8,128)(2,1)S(1)}, u32[]{:S(2)}, u32[]{:S(2)}) collective-permute-start(bf16[256,384]{1,0:T(8,128)(2,1)S(1)} %collective-permute-done.9), channel_id=1, source_target_pairs={{0,1},{1,2},{2,3},{3,4},{4,5},{5,6},{6,7},{7,0},{8,9},{9,10},{10,1... | collective-permute-start | bytes 589832 | tf_op jit(solution)/shard_map/ppermute | solution.py:16
  82.1 0.7 constant_dynamic-update-slice_fusion.14
  82.8 0.7 constant_dynamic-update-slice_fusion.6
  83.5 2.3 %collective-permute-start.12 = (bf16[256,384]{1,0:T(8,128)(2,1)S(1)}, bf16[256,384]{1,0:T(8,128)(2,1)S(1)}, u32[]{:S(2)}, u32[]{:S(2)}) collective-permute-start(bf16[256,384]{1,0:T(8,128)(2,1)S(1)} %collective-permute-done.10), channel_id=1, source_target_pairs={{0,7},{1,0},{2,1},{3,2},{4,3},{5,4},{6,5},{7,6},{8,15},{9,8},{10,9... | collective-permute-start | bytes 589832 | tf_op jit(solution)/shard_map/ppermute | solution.py:21
  85.8 0.7 constant_dynamic-update-slice_fusion.13
  86.5 0.7 constant_dynamic-update-slice_fusion.5
  87.2 4.0 %collective-permute-done.5 = bf16[256,384]{1,0:T(8,128)(2,1)S(1)} collective-permute-done((bf16[256,384]{1,0:T(8,128)(2,1)S(1)}, bf16[256,384]{1,0:T(8,128)(2,1)S(1)}, u32[]{:S(2)}, u32[]{:S(2)}) %collective-permute-start.5) | collective-permute-done | bytes 196640 | tf_op jit(solution)/shard_map/ppermute | solution.py:21
  91.1 4.3 %collective-permute-start.7 = (bf16[256,384]{1,0:T(8,128)(2,1)S(1)}, bf16[256,384]{1,0:T(8,128)(2,1)S(1)}, u32[]{:S(2)}, u32[]{:S(2)}) collective-permute-start(bf16[256,384]{1,0:T(8,128)(2,1)S(1)} %collective-permute-done.5), channel_id=1, source_target_pairs={{0,7},{1,0},{2,1},{3,2},{4,3},{5,4},{6,5},{7,6},{8,15},{9,8},{10,9... | collective-permute-start | bytes 589832 | tf_op jit(solution)/shard_map/ppermute | solution.py:21
  95.5 0.7 constant_dynamic-update-slice_fusion.12
  96.2 0.7 constant_dynamic-update-slice_fusion.4
  96.9 2.7 %collective-permute-done.12 = bf16[256,384]{1,0:T(8,128)(2,1)S(1)} collective-permute-done((bf16[256,384]{1,0:T(8,128)(2,1)S(1)}, bf16[256,384]{1,0:T(8,128)(2,1)S(1)}, u32[]{:S(2)}, u32[]{:S(2)}) %collective-permute-start.12) | collective-permute-done | bytes 196640 | tf_op jit(solution)/shard_map/ppermute | solution.py:21
  99.6 4.3 %collective-permute-start.14 = (bf16[256,384]{1,0:T(8,128)(2,1)S(1)}, bf16[256,384]{1,0:T(8,128)(2,1)S(1)}, u32[]{:S(2)}, u32[]{:S(2)}) collective-permute-start(bf16[256,384]{1,0:T(8,128)(2,1)S(1)} %collective-permute-done.12), channel_id=1, source_target_pairs={{0,7},{1,0},{2,1},{3,2},{4,3},{5,4},{6,5},{7,6},{8,15},{9,8},{10,9... | collective-permute-start | bytes 589832 | tf_op jit(solution)/shard_map/ppermute | solution.py:21
  103.8 0.7 constant_dynamic-update-slice_fusion.11
  104.6 0.7 constant_dynamic-update-slice_fusion.3
  105.3 3.9 %collective-permute-done.13 = bf16[256,384]{1,0:T(8,128)(2,1)} collective-permute-done((bf16[256,384]{1,0:T(8,128)(2,1)S(1)}, bf16[256,384]{1,0:T(8,128)(2,1)}, u32[]{:S(2)}, u32[]{:S(2)}) %collective-permute-start.13) | collective-permute-done | bytes 196640 | tf_op jit(solution)/shard_map/ppermute | solution.py:16
  109.1 2.6 %collective-permute-start.15 = (bf16[256,384]{1,0:T(8,128)(2,1)}, bf16[256,384]{1,0:T(8,128)(2,1)}, u32[]{:S(2)}, u32[]{:S(2)}) collective-permute-start(bf16[256,384]{1,0:T(8,128)(2,1)} %collective-permute-done.13), channel_id=1, source_target_pairs={{0,1},{1,2},{2,3},{3,4},{4,5},{5,6},{6,7},{7,0},{8,9},{9,10},{10,1... | collective-permute-start | bytes 589832 | tf_op jit(solution)/shard_map/ppermute | solution.py:16
  111.7 0.7 constant_dynamic-update-slice_fusion.10
  112.4 1.6 %constant_dynamic-update-slice_fusion.2 = bf16[2048,384]{1,0:T(8,128)(2,1)} fusion(bf16[2048,384]{1,0:T(8,128)(2,1)} %constant_dynamic-update-slice_fusion.3, bf16[256,384]{1,0:T(8,128)(2,1)} %collective-permute-done.13, s32[]{:T(128)S(6)} %select_n.103), kind=kLoop, calls=%fused_computation.311 | loop fusion | bytes 393220 | tf_op jit(solution)/shard_map/dynamic_update_slice | solution.py:17
  114.1 0.7 constant_dynamic-update-slice_fusion.9
  114.8 4.6 %collective-permute-done.14 = bf16[256,384]{1,0:T(8,128)(2,1)S(1)} collective-permute-done((bf16[256,384]{1,0:T(8,128)(2,1)S(1)}, bf16[256,384]{1,0:T(8,128)(2,1)S(1)}, u32[]{:S(2)}, u32[]{:S(2)}) %collective-permute-start.14) | collective-permute-done | bytes 196640 | tf_op jit(solution)/shard_map/ppermute | solution.py:21
  119.4 0.7 constant_dynamic-update-slice_fusion.1
  120.1 0.7 constant_dynamic-update-slice_fusion.8
  121.0 3.1 %fusion.204 = (f32[256]{0:T(256)S(1)}, f32[256,2048]{1,0:T(8,128)S(1)}) fusion(bf16[256,384]{1,0:T(8,128)(2,1)S(1)} %convolution_convert_fusion.5, bf16[2048,384]{1,0:T(8,128)(2,1)} %constant_dynamic-update-slice_fusion.8, bf16[384,384]{1,0:T(8,128)(2,1)S(1)} %copy-done), kind=kOutput, calls=%fused_computation.338 | convolution fusion | flops 1008467712 | bytes 4162560 | tf_op jit(solution)/shard_map/qc,kc->qk/dot_general | solution.py:108
  124.2 0.4 fusion
  124.6 3.1 %fusion.15 = bf16[256,384]{1,0:T(8,128)(2,1)S(1)} fusion(bf16[2048,384]{1,0:T(8,128)(2,1)} %constant_dynamic-update-slice_fusion.8, bf16[384,384]{1,0:T(8,128)(2,1)} %param.20, f32[256,2048]{1,0:T(8,128)S(1)} %get-tuple-element.35, f32[256]{0:T(256)S(1)} %get-tuple-element.34, f32[256]{0:T(256)S(1)} %fusion), kind=kOutput, calls=%fused_computation.82 | convolution fusion | flops 1008664576 | bytes 4163584 | tf_op jit(solution)/shard_map/dot_general | solution.py:114
  127.8 0.9 convolution_convert_fusion.4
  128.7 1.6 %constant_dynamic-update-slice_fusion = bf16[2048,384]{1,0:T(8,128)(2,1)} fusion(bf16[2048,384]{1,0:T(8,128)(2,1)} %constant_dynamic-update-slice_fusion.1, bf16[256,384]{1,0:T(8,128)(2,1)} %collective-permute-done.15, s32[]{:T(128)S(6)} %select_n.107), kind=kLoop, calls=%fused_computation.309 | loop fusion | bytes 393220 | tf_op jit(solution)/shard_map/dynamic_update_slice | solution.py:17
  130.3 3.3 %fusion.203 = (f32[256]{0:T(256)S(1)}, f32[256,2048]{1,0:T(8,128)S(1)}) fusion(bf16[256,384]{1,0:T(8,128)(2,1)} %convolution_convert_fusion.4, bf16[2048,384]{1,0:T(8,128)(2,1)} %constant_dynamic-update-slice_fusion, bf16[384,384]{1,0:T(8,128)(2,1)S(1)} %copy-done), kind=kOutput, calls=%fused_computation.337 | convolution fusion | flops 1008467712 | bytes 4162560 | tf_op jit(solution)/shard_map/qc,kc->qk/dot_general | solution.py:108
  133.6 0.4 fusion.2
  134.1 3.2 %fusion.13 = bf16[256,384]{1,0:T(8,128)(2,1)S(1)} fusion(bf16[2048,384]{1,0:T(8,128)(2,1)} %constant_dynamic-update-slice_fusion, bf16[384,384]{1,0:T(8,128)(2,1)} %param.20, f32[256,2048]{1,0:T(8,128)S(1)} %get-tuple-element.33, f32[256]{0:T(256)S(1)} %get-tuple-element.32, f32[256]{0:T(256)S(1)} %fusion.2), kind=kOutput, calls=%fused_computation.80 | convolution fusion | flops 1008664576 | bytes 4163584 | tf_op jit(solution)/shard_map/dot_general | solution.py:114
  137.9 0.8 pad_maximum_fusion.2
  (102 shorter events, 14.4 us)
Async XLA Ops:
  6.5 114.5 %copy-start = (bf16[384,384]{1,0:T(8,128)(2,1)S(1)}, bf16[384,384]{1,0:T(8,128)(2,1)}, u32[]{:S(2)}) copy-start(bf16[384,384]{1,0:T(8,128)(2,1)} %param.19) | copy-start | bytes 884740
  6.5 28.9 %all-gather.2.cloned.1.call-start = ((), (), s32[]{:S(2)}) async-start(), calls=%async_computation | async-start | bytes 2359296 | tf_op jit(solution)/shard_map/all_gather | solution.py:66
  9.1 14.4 %copy-start.6 = (s32[2,2]{1,0:T(2,128)S(1)}, s32[2,2]{1,0:T(2,128)}, u32[]{:S(2)}) copy-start(s32[2,2]{1,0:T(2,128)} %param.13) | copy-start | bytes 52
  9.1 9.1 %collective-permute-start = (bf16[2,1,128,384]{3,2,1,0:T(8,128)(2,1)S(1)}, bf16[2,1,128,384]{3,2,1,0:T(8,128)(2,1)S(1)}, u32[]{:S(2)}, u32[]{:S(2)}) collective-permute-start(bf16[2,1,128,384]{3,2,1,0:T(8,128)(2,1)S(1)} %get-tuple-element.26), channel_id=1, source_target_pairs={{0,1},{1,2},{2,3},{3,4},{4,5},{5,6},{6,7},{8,9},{9,10},{10,11},{11... | collective-permute-start | bytes 589832 | tf_op jit(solution)/shard_map/ppermute | solution.py:36
  14.0 8.3 %collective-permute-start.1 = (bf16[2,1,128,384]{3,2,1,0:T(8,128)(2,1)S(1)}, bf16[2,1,128,384]{3,2,1,0:T(8,128)(2,1)S(1)}, u32[]{:S(2)}, u32[]{:S(2)}) collective-permute-start(bf16[2,1,128,384]{3,2,1,0:T(8,128)(2,1)S(1)} %get-tuple-element.27), channel_id=1, source_target_pairs={{1,0},{2,1},{3,2},{4,3},{5,4},{6,5},{7,6},{9,8},{10,9},{11,10},{12... | collective-permute-start | bytes 589832 | tf_op jit(solution)/shard_map/ppermute | solution.py:38
  23.3 1.1 copy-start.1
  40.6 1.5 %copy-start.2 = (bf16[2,4,130,384]{3,2,1,0:T(8,128)(2,1)S(1)}, bf16[2,4,130,384]{3,2,1,0:T(8,128)(2,1)}, u32[]{:S(2)}) copy-start(bf16[2,4,130,384]{3,2,1,0:T(8,128)(2,1)} %gather_fusion) | copy-start | bytes 2396164
  40.6 5.1 %slice-start = ((s8[7962624]{0:T(1024)(128)(4,1)}), s8[4194304]{0:T(1024)(128)(4,1)S(1)}, s32[]{:S(2)}) async-start(s8[7962624]{0:T(1024)(128)(4,1)} %bitcast.403), calls=%async_computation.1 | async-start | bytes 8388608
  42.3 3.4 %slice-start.1 = ((s8[7962624]{0:T(1024)(128)(4,1)}), s8[3768320]{0:T(1024)(128)(4,1)S(1)}, s32[]{:S(2)}) async-start(s8[7962624]{0:T(1024)(128)(4,1)} %bitcast.403), calls=%async_computation.2 | async-start | bytes 7536640
  51.9 1.0 copy-start.3
  51.9 1.0 copy-start.8
  52.2 1.1 copy-start.7
  53.5 21.3 %collective-permute-start.2 = (bf16[256,384]{1,0:T(8,128)(2,1)S(1)}, bf16[256,384]{1,0:T(8,128)(2,1)S(1)}, u32[]{:S(2)}, u32[]{:S(2)}) collective-permute-start(bf16[256,384]{1,0:T(8,128)(2,1)S(1)} %bitcast.405), channel_id=1, source_target_pairs={{0,1},{1,2},{2,3},{3,4},{4,5},{5,6},{6,7},{7,0},{8,9},{9,10},{10,1... | collective-permute-start | bytes 589832 | tf_op jit(solution)/shard_map/ppermute | solution.py:16
  55.2 19.6 %collective-permute-start.3 = (bf16[256,384]{1,0:T(8,128)(2,1)S(1)}, bf16[256,384]{1,0:T(8,128)(2,1)S(1)}, u32[]{:S(2)}, u32[]{:S(2)}) collective-permute-start(bf16[256,384]{1,0:T(8,128)(2,1)S(1)} %bitcast.406), channel_id=1, source_target_pairs={{0,7},{1,0},{2,1},{3,2},{4,3},{5,4},{6,5},{7,6},{8,15},{9,8},{10,9... | collective-permute-start | bytes 589832 | tf_op jit(solution)/shard_map/ppermute | solution.py:21
  66.1 13.6 %collective-permute-start.9 = (bf16[256,384]{1,0:T(8,128)(2,1)S(1)}, bf16[256,384]{1,0:T(8,128)(2,1)S(1)}, u32[]{:S(2)}, u32[]{:S(2)}) collective-permute-start(bf16[256,384]{1,0:T(8,128)(2,1)S(1)} %bitcast.409), channel_id=1, source_target_pairs={{0,1},{1,2},{2,3},{3,4},{4,5},{5,6},{6,7},{7,0},{8,9},{9,10},{10,1... | collective-permute-start | bytes 589832 | tf_op jit(solution)/shard_map/ppermute | solution.py:16
  66.1 17.4 %collective-permute-start.10 = (bf16[256,384]{1,0:T(8,128)(2,1)S(1)}, bf16[256,384]{1,0:T(8,128)(2,1)S(1)}, u32[]{:S(2)}, u32[]{:S(2)}) collective-permute-start(bf16[256,384]{1,0:T(8,128)(2,1)S(1)} %bitcast.410), channel_id=1, source_target_pairs={{0,7},{1,0},{2,1},{3,2},{4,3},{5,4},{6,5},{7,6},{8,15},{9,8},{10,9... | collective-permute-start | bytes 589832 | tf_op jit(solution)/shard_map/ppermute | solution.py:21
  74.8 12.4 %collective-permute-start.4 = (bf16[256,384]{1,0:T(8,128)(2,1)S(1)}, bf16[256,384]{1,0:T(8,128)(2,1)S(1)}, u32[]{:S(2)}, u32[]{:S(2)}) collective-permute-start(bf16[256,384]{1,0:T(8,128)(2,1)S(1)} %collective-permute-done.2), channel_id=1, source_target_pairs={{0,1},{1,2},{2,3},{3,4},{4,5},{5,6},{6,7},{7,0},{8,9},{9,10},{10,1... | collective-permute-start | bytes 589832 | tf_op jit(solution)/shard_map/ppermute | solution.py:16
  74.8 16.3 %collective-permute-start.5 = (bf16[256,384]{1,0:T(8,128)(2,1)S(1)}, bf16[256,384]{1,0:T(8,128)(2,1)S(1)}, u32[]{:S(2)}, u32[]{:S(2)}) collective-permute-start(bf16[256,384]{1,0:T(8,128)(2,1)S(1)} %collective-permute-done.3), channel_id=1, source_target_pairs={{0,7},{1,0},{2,1},{3,2},{4,3},{5,4},{6,5},{7,6},{8,15},{9,8},{10,9... | collective-permute-start | bytes 589832 | tf_op jit(solution)/shard_map/ppermute | solution.py:21
  79.6 15.8 %collective-permute-start.11 = (bf16[256,384]{1,0:T(8,128)(2,1)S(1)}, bf16[256,384]{1,0:T(8,128)(2,1)S(1)}, u32[]{:S(2)}, u32[]{:S(2)}) collective-permute-start(bf16[256,384]{1,0:T(8,128)(2,1)S(1)} %collective-permute-done.9), channel_id=1, source_target_pairs={{0,1},{1,2},{2,3},{3,4},{4,5},{5,6},{6,7},{7,0},{8,9},{9,10},{10,1... | collective-permute-start | bytes 589832 | tf_op jit(solution)/shard_map/ppermute | solution.py:16
  83.5 16.0 %collective-permute-start.12 = (bf16[256,384]{1,0:T(8,128)(2,1)S(1)}, bf16[256,384]{1,0:T(8,128)(2,1)S(1)}, u32[]{:S(2)}, u32[]{:S(2)}) collective-permute-start(bf16[256,384]{1,0:T(8,128)(2,1)S(1)} %collective-permute-done.10), channel_id=1, source_target_pairs={{0,7},{1,0},{2,1},{3,2},{4,3},{5,4},{6,5},{7,6},{8,15},{9,8},{10,9... | collective-permute-start | bytes 589832 | tf_op jit(solution)/shard_map/ppermute | solution.py:21
  87.2 18.1 %collective-permute-start.6 = (bf16[256,384]{1,0:T(8,128)(2,1)S(1)}, bf16[256,384]{1,0:T(8,128)(2,1)S(1)}, u32[]{:S(2)}, u32[]{:S(2)}) collective-permute-start(bf16[256,384]{1,0:T(8,128)(2,1)S(1)} %collective-permute-done.4), channel_id=1, source_target_pairs={{0,1},{1,2},{2,3},{3,4},{4,5},{5,6},{6,7},{7,0},{8,9},{9,10},{10,1... | collective-permute-start | bytes 589832 | tf_op jit(solution)/shard_map/ppermute | solution.py:16
  91.1 22.9 %collective-permute-start.7 = (bf16[256,384]{1,0:T(8,128)(2,1)S(1)}, bf16[256,384]{1,0:T(8,128)(2,1)S(1)}, u32[]{:S(2)}, u32[]{:S(2)}) collective-permute-start(bf16[256,384]{1,0:T(8,128)(2,1)S(1)} %collective-permute-done.5), channel_id=1, source_target_pairs={{0,7},{1,0},{2,1},{3,2},{4,3},{5,4},{6,5},{7,6},{8,15},{9,8},{10,9... | collective-permute-start | bytes 589832 | tf_op jit(solution)/shard_map/ppermute | solution.py:21
  95.5 13.7 %collective-permute-start.13 = (bf16[256,384]{1,0:T(8,128)(2,1)S(1)}, bf16[256,384]{1,0:T(8,128)(2,1)}, u32[]{:S(2)}, u32[]{:S(2)}) collective-permute-start(bf16[256,384]{1,0:T(8,128)(2,1)S(1)} %collective-permute-done.11), channel_id=1, source_target_pairs={{0,1},{1,2},{2,3},{3,4},{4,5},{5,6},{6,7},{7,0},{8,9},{9,10},{10,1... | collective-permute-start | bytes 589832 | tf_op jit(solution)/shard_map/ppermute | solution.py:16
  96.2 24.6 %copy-start.5 = (bf16[384,384]{1,0:T(8,128)(2,1)S(1)}, bf16[384,384]{1,0:T(8,128)(2,1)}, u32[]{:S(2)}) copy-start(bf16[384,384]{1,0:T(8,128)(2,1)} %param.18) | copy-start | bytes 884740
  99.6 19.8 %collective-permute-start.14 = (bf16[256,384]{1,0:T(8,128)(2,1)S(1)}, bf16[256,384]{1,0:T(8,128)(2,1)S(1)}, u32[]{:S(2)}, u32[]{:S(2)}) collective-permute-start(bf16[256,384]{1,0:T(8,128)(2,1)S(1)} %collective-permute-done.12), channel_id=1, source_target_pairs={{0,7},{1,0},{2,1},{3,2},{4,3},{5,4},{6,5},{7,6},{8,15},{9,8},{10,9... | collective-permute-start | bytes 589832 | tf_op jit(solution)/shard_map/ppermute | solution.py:21
  105.3 14.8 %collective-permute-start.8 = (bf16[256,384]{1,0:T(8,128)(2,1)S(1)}, bf16[256,384]{1,0:T(8,128)(2,1)S(1)}, u32[]{:S(2)}, u32[]{:S(2)}) collective-permute-start(bf16[256,384]{1,0:T(8,128)(2,1)S(1)} %collective-permute-done.6), channel_id=1, source_target_pairs={{0,1},{1,2},{2,3},{3,4},{4,5},{5,6},{6,7},{7,0},{8,9},{9,10},{10,1... | collective-permute-start | bytes 589832 | tf_op jit(solution)/shard_map/ppermute | solution.py:16
  109.1 19.6 %collective-permute-start.15 = (bf16[256,384]{1,0:T(8,128)(2,1)}, bf16[256,384]{1,0:T(8,128)(2,1)}, u32[]{:S(2)}, u32[]{:S(2)}) collective-permute-start(bf16[256,384]{1,0:T(8,128)(2,1)} %collective-permute-done.13), channel_id=1, source_target_pairs={{0,1},{1,2},{2,3},{3,4},{4,5},{5,6},{6,7},{7,0},{8,9},{9,10},{10,1... | collective-permute-start | bytes 589832 | tf_op jit(solution)/shard_map/ppermute | solution.py:16
  134.0 3.2 %copy-start.4 = (bf16[384,384]{1,0:T(8,128)(2,1)S(1)}, bf16[384,384]{1,0:T(8,128)(2,1)}, u32[]{:S(2)}) copy-start(bf16[384,384]{1,0:T(8,128)(2,1)} %param.21) | copy-start | bytes 884740
Sparse Core Ops, SparseCore 0:
  23.4 12.0 all-gather.1
